TPU v7x, 32 devices: a whole 2x2x4 slice. The times are simulated.
32 devices in a mesh: member: 4 (over y, core), band: 8 (over z, x).
Axes of the slice: x: 2, y: 2, z: 4, core: 2. Of those that a mesh axis runs over, the one named last changes fastest.
Arguments:
- obs_values: bfloat16 [65536, 128], P(('member', 'band')), parts along dimension 0, may hold values from -6 to 6
- obs_band: int32 [65536, 1], P(('member', 'band')), parts along dimension 0, may hold values from 0 to 7; in each aligned block of 2048 rows (0 to 2047, 2048 to 4095, ...) at most 256 rows name the same one
- obs_cell: int32 [65536], P(('member', 'band')), parts along dimension 0, may hold values from 0 to 2047
- obs_offset: int32 [65536], P(('member', 'band')), parts along dimension 0, may hold values from 0 to 7
- sat_values: bfloat16 [65536, 128], P(('member', 'band')), parts along dimension 0, may hold values from -6 to 6
- sat_cell: int32 [65536], P(('member', 'band')), parts along dimension 0, may hold values from 0 to 2047
- sat_offset: int32 [65536], P(('member', 'band')), parts along dimension 0, may hold values from 0 to 7
- density_embed: float32 [128], replicated, may hold values from -3 to 3
- conv1_weight: bfloat16 [3, 3, 128, 128], replicated, may hold values from -0.1875 to 0.1875
- conv1_bias: float32 [128], replicated, may hold values from -3 to 3
- conv2_weight: bfloat16 [3, 3, 128, 256], replicated, may hold values from -0.1875 to 0.1875
- conv2_bias: float32 [256], replicated, may hold values from -3 to 3
- proj_weight: bfloat16 [256, 256], replicated, may hold values from -0.375 to 0.375
Outputs:
- latents: bfloat16 [64, 64, 256], P('member'), parts along dimension 0
There are 4 independent parts, one for each index of `member`. A program takes and returns all parts, laid end to end along the dimension named above; an argument that names none is the same for every part. Nothing has to cross between parts.
Inputs may be any that keep to these rules, and one draw needn't show every extreme that they name: `obs_band`: among the station rows of one device, at most 256 name the same band, and in every draw some band is named by exactly 256 rows of some device.
All inputs are finite; a program needn't handle non-finite values.
Results may differ from a plain program's by a relative error of at most 0.0061.
Values may be sent and summed in bfloat16 or wider, within the bound.
No kernel may reach another device: no remote copies, remote signals or barrier semaphores. Data moves between devices by JAX's collectives and lax.ppermute only.
A program may use at most 64 MiB of HBM per device.

v0:
```python
import jax
import jax.numpy as jnp
from jax import lax
from jax.sharding import PartitionSpec as P

LAT_DEV = 8
LON = 256
META = 16


def passed_along(value, axis, by):
    length = lax.axis_size(axis)
    pairs = [(i, i + by) for i in range(length) if 0 <= i + by < length]
    return lax.ppermute(value, axis, pairs)


def weights_of(offsets):
    return jnp.exp(-offsets.astype(jnp.float32) ** 2 / 32.0).astype(jnp.bfloat16)


def deposit(values, cells, weight, total_cells):
    block = min(512, total_cells)
    count = total_cells // block

    def one_block(start):
        ids = start + jnp.arange(block, dtype=jnp.int32)
        table = jnp.where(
            ids[:, None] == cells[None, :], weight[None, :], jnp.zeros((), jnp.bfloat16)
        )
        sums = jnp.dot(table, values, preferred_element_type=jnp.float32)
        density = jnp.sum(table, axis=1, dtype=jnp.float32)
        return (sums, density)

    starts = jnp.arange(count, dtype=jnp.int32) * block
    sums, density = lax.map(one_block, starts)
    return (sums.reshape(total_cells, values.shape[1]), density.reshape(total_cells))


def strided(padded, weight, bias):
    count, width, chans = padded.shape
    grid = jnp.pad(padded, ((0, 1), (1, 1), (0, 0)))
    parted = grid.reshape((count + 1) // 2, 2, (width + 2) // 2, 2, chans)
    rows = (count - 1) // 2
    cols = width // 2
    total = jnp.zeros((rows * cols, weight.shape[3]), jnp.float32)
    for first in range(3):
        for second in range(3):
            piece = parted[
                first // 2 : first // 2 + rows,
                first % 2,
                second // 2 : second // 2 + cols,
                second % 2,
                :,
            ]
            total = total + jnp.dot(
                piece.reshape(rows * cols, chans),
                weight[first, second],
                preferred_element_type=jnp.float32,
            )
    return jax.nn.gelu(total + bias, approximate=False).reshape(rows, cols, weight.shape[3])


def project(latent, proj_weight):
    flat = jnp.dot(
        latent.reshape(-1, latent.shape[2]), proj_weight, preferred_element_type=jnp.float32
    )
    return flat.astype(jnp.bfloat16).reshape(latent.shape)


def route(obs_values, obs_band, obs_cell, obs_offset, bands):
    obs_rows, d_in = obs_values.shape
    capacity = obs_rows // 8
    slots = bands * capacity
    target = obs_band[:, 0]
    choose = (target[:, None] == jnp.arange(bands, dtype=jnp.int32)[None, :]).astype(jnp.bfloat16)
    earlier = (
        jnp.arange(obs_rows, dtype=jnp.int32)[:, None]
        > jnp.arange(obs_rows, dtype=jnp.int32)[None, :]
    ).astype(jnp.bfloat16)
    before = jnp.dot(earlier, choose, preferred_element_type=jnp.float32)
    rank = jnp.sum(before * choose.astype(jnp.float32), axis=1).astype(jnp.int32)
    position = target * capacity + rank
    table = (jnp.arange(slots, dtype=jnp.int32)[:, None] == position[None, :]).astype(jnp.bfloat16)
    sent = jnp.dot(table, obs_values, preferred_element_type=jnp.float32).astype(jnp.bfloat16)
    meta = jnp.stack([obs_cell // 64, obs_cell % 64, obs_offset + 1], axis=0).astype(jnp.bfloat16)
    meta_sent = jnp.dot(meta, table.T, preferred_element_type=jnp.float32).astype(jnp.bfloat16)
    meta_sent = meta_sent.reshape(3, bands, capacity).transpose(1, 0, 2)
    meta_sent = meta_sent.reshape(bands, 3 * capacity // d_in, d_in)
    pad = jnp.zeros((bands, META - 3 * capacity // d_in, d_in), jnp.bfloat16)
    packet = jnp.concatenate([sent.reshape(bands, capacity, d_in), meta_sent, pad], axis=1)
    got = lax.all_to_all(packet, "band", split_axis=0, concat_axis=0, tiled=True)
    got_values = got[:, :capacity, :].reshape(slots, d_in)
    got_meta = got[:, capacity : capacity + 3 * capacity // d_in, :]
    got_meta = got_meta.reshape(bands, 3, capacity).transpose(1, 0, 2).reshape(3, slots)
    got_meta = got_meta.astype(jnp.int32)
    cells = got_meta[0] * 64 + got_meta[1]
    weight = jnp.where(got_meta[2] > 0, weights_of(got_meta[2] - 1), jnp.zeros((), jnp.bfloat16))
    return (got_values, cells, weight)


def body(
    obs_values,
    obs_band,
    obs_cell,
    obs_offset,
    sat_values,
    sat_cell,
    sat_offset,
    density_embed,
    conv1_weight,
    conv1_bias,
    conv2_weight,
    conv2_bias,
    proj_weight,
):
    bands = lax.axis_size("band")
    position_index = lax.axis_index("band")
    d_in = obs_values.shape[1]
    band_cells = LAT_DEV * LON
    got_values, got_cells, got_weight = route(obs_values, obs_band, obs_cell, obs_offset, bands)
    sat_sums, sat_density = deposit(sat_values, sat_cell, weights_of(sat_offset), band_cells)
    sta_sums, sta_density = deposit(got_values, got_cells, got_weight, band_cells)
    sums = sat_sums + sta_sums
    density = sat_density + sta_density
    grid0 = sums / jnp.maximum(density, 1.0)[:, None] + density[:, None] * density_embed[None, :]
    grid0 = grid0.astype(jnp.bfloat16).reshape(LAT_DEV, LON, d_in)
    above = passed_along(grid0[-3:], "band", 1)
    hidden1 = strided(jnp.concatenate([above, grid0], axis=0), conv1_weight, conv1_bias)
    keep_rows = (jnp.arange(hidden1.shape[0]) > 0) | (position_index > 0)
    hidden1 = jnp.where(keep_rows[:, None, None], hidden1, 0.0).astype(jnp.bfloat16)
    latent = strided(hidden1, conv2_weight, conv2_bias).astype(jnp.bfloat16)
    mine = project(latent, proj_weight)
    full = jnp.zeros((bands,) + mine.shape, mine.dtype)
    full = lax.dynamic_update_slice(full, mine[None], (position_index, 0, 0, 0))
    gathered = lax.psum(full, "band")
    return gathered.reshape((bands * mine.shape[0],) + mine.shape[1:])


def solution(mesh):
    placed = (
        P(("member", "band"), None),
        P(("member", "band"), None),
        P(("member", "band")),
        P(("member", "band")),
        P(("member", "band"), None),
        P(("member", "band")),
        P(("member", "band")),
        P(),
        P(),
        P(),
        P(),
        P(),
        P(),
    )
    return jax.shard_map(
        body, mesh=mesh, in_specs=placed, out_specs=P("member", None, None), check_vma=False
    )
```

profile of v0, /device:TPU:0, one launch (start us, length us, event | category | flops | bytes accessed | tf_op | source)
XLA Modules:
  0.0 151.4 jit_solution(4917465896632138708)
XLA Ops:
  6.5 2.2 %fusion.30 = f32[2048]{0:T(1024)S(1)} fusion(s32[2048]{0:T(1024)} %bitcast.178), kind=kOutput, calls=%fused_computation.58 | convolution fusion | flops 71399424 | bytes 16384 | tf_op jit(solution)/shard_map/dot_general | solution.py:80
  8.9 2.9 %fusion.23 = bf16[3,2048]{1,0:T(4,128)(2,1)S(1)} fusion(s32[2048]{0:T(1024)S(1)} %convert_add_fusion, bf16[1,2048]{1,0:T(2,128)(2,1)S(1)} %stack.18, bf16[1,2048]{1,0:T(2,128)(2,1)S(1)} %stack.17, bf16[1,2048]{1,0:T(2,128)(2,1)S(1)} %stack.16), kind=kOutput, calls=%fused_computation.33 | convolution fusion | flops 29403136 | bytes 32768 | tf_op jit(solution)/shard_map/dot_general | solution.py:86
  11.8 3.0 %fusion.21 = bf16[2048,128]{1,0:T(8,128)(2,1)S(1)} fusion(bf16[2048,128]{1,0:T(8,128)(2,1)S(1)} %copy-done, s32[2048]{0:T(1024)S(1)} %convert_add_fusion), kind=kOutput, calls=%fused_computation.31 | convolution fusion | flops 1078198272 | bytes 1056768 | tf_op jit(solution)/shard_map/dot_general | solution.py:84
  14.9 1.0 maximum_maximum_fusion
  15.9 7.4 %all-to-all-start = ((bf16[8,272,128]{2,1,0:T(8,128)(2,1)}), bf16[8,272,128]{2,1,0:T(8,128)(2,1)S(1)}, u32[]{:S(2)}, u32[]{:S(2)}) async-start(bf16[8,272,128]{2,1,0:T(8,128)(2,1)} %maximum_maximum_fusion), calls=%async_computation | async-start | bytes 1114112 | tf_op jit(solution)/shard_map/all_to_all | solution.py:91
  23.5 10.4 %while.24 = (s32[]{:T(128)}, f32[4,512,128]{2,1,0:T(8,128)S(1)}, f32[4,512]{1,0:T(4,128)S(1)}, s32[4]{0:T(128)S(1)}, s32[2048]{0:T(1024)S(1)}, /*index=5*/bf16[2...) while((s32[]{:T(128)}, f32[4,512,128]{2,1,0:T(8,128)S(1)}, ...), condition=%wide.region_2.3_spmd, body=%wide.region_0.2_spmd.sunk | while | flops 274726912 | bytes 823413 | solution.py:35
  23.5 0.6 dynamic_slice.9
  24.1 0.6 iota_add_fusion.4
  24.7 0.8 fusion.198
  25.5 0.5 convert_reduce_fusion.4
  26.1 0.6 dynamic_slice.9
  26.7 0.6 iota_add_fusion.4
  27.3 0.8 fusion.198
  28.1 0.5 convert_reduce_fusion.4
  28.7 0.6 dynamic_slice.9
  29.3 0.6 iota_add_fusion.4
  29.9 0.8 fusion.198
  30.7 0.5 convert_reduce_fusion.4
  31.3 0.6 dynamic_slice.9
  31.9 0.6 iota_add_fusion.4
  32.5 0.8 fusion.198
  33.3 0.5 convert_reduce_fusion.4
  33.9 4.6 %all-to-all-done = bf16[8,272,128]{2,1,0:T(8,128)(2,1)S(1)} async-done(((bf16[8,272,128]{2,1,0:T(8,128)(2,1)}), bf16[8,272,128]{2,1,0:T(8,128)(2,1)S(1)}, u32[]{:S(2)}, u32[]{:S(2)}) %all-to-all-start) | async-done | bytes 557088 | tf_op jit(solution)/shard_map/all_to_all | solution.py:91
  38.8 10.5 %while.25 = (s32[]{:T(128)}, f32[4,512,128]{2,1,0:T(8,128)S(1)}, f32[4,512]{1,0:T(4,128)S(1)}, s32[4]{0:T(128)S(1)}, s32[2048]{0:T(1024)S(1)}, /*index=5*/bf16[2...) while((s32[]{:T(128)}, f32[4,512,128]{2,1,0:T(8,128)S(1)}, ...), condition=%wide.region_6.7_spmd, body=%wide.region_4.6_spmd.sunk | while | flops 274726912 | bytes 823413 | solution.py:35
  38.8 0.6 dynamic_slice.10
  39.4 0.6 iota_add_fusion.5
  40.0 0.8 fusion.200
  40.8 0.5 convert_reduce_fusion.5
  41.4 0.6 dynamic_slice.10
  42.0 0.6 iota_add_fusion.5
  42.7 0.8 fusion.200
  43.4 0.5 convert_reduce_fusion.5
  44.0 0.6 dynamic_slice.10
  44.7 0.6 iota_add_fusion.5
  45.3 0.8 fusion.200
  46.7 0.6 dynamic_slice.10
  47.3 0.6 iota_add_fusion.5
  47.9 0.8 fusion.200
  50.3 3.6 %collective-permute-start = (bf16[3,256,128]{2,1,0:T(8,128)(2,1)S(1)}, bf16[3,256,128]{2,1,0:T(8,128)(2,1)S(1)}, u32[]{:S(2)}, u32[]{:S(2)}) collective-permute-start(bf16[3,256,128]{2,1,0:T(8,128)(2,1)S(1)} %bitcast.157), channel_id=1, source_target_pairs={{0,1},{1,2},{2,3},{3,4},{4,5},{5,6},{6,7},{8,9},{9,10},{10,11},{11... | collective-permute-start | bytes 589832 | tf_op jit(solution)/shard_map/ppermute | solution.py:14
  53.9 0.7 add_convert_fusion
  54.6 2.5 %collective-permute-done = bf16[3,256,128]{2,1,0:T(8,128)(2,1)S(1)} collective-permute-done((bf16[3,256,128]{2,1,0:T(8,128)(2,1)S(1)}, bf16[3,256,128]{2,1,0:T(8,128)(2,1)S(1)}, u32[]{:S(2)}, u32[]{:S(2)}) %collective-permute-start) | collective-permute-done | bytes 196640 | tf_op jit(solution)/shard_map/ppermute | solution.py:14
  57.6 3.2 %fusion.169 = (bf16[5,1,128,1,128]{4,3,2,1,0:T(2,128)(2,1)S(1)}, bf16[5,1,128,1,128]{4,3,2,1,0:T(2,128)(2,1)S(1)}, bf16[5,1,128,1,128]{4,3,2,1,0:T(2,128)(2,1)S(...) fusion(bf16[6,2,129,2,128]{4,3,2,1,0:T(2,128)(2,1)S(1)} %reshap, ...), kind=kLoop, calls=%fused_computation.236 | loop fusion | bytes 2949120 | tf_op jit(solution)/shard_map/slice | solution.py:48
  61.1 0.8 copy-done.3
  63.7 0.9 fusion.37
  67.3 0.6 convolution_convert_fusion
  67.9 0.8 copy-done.1
  68.7 74.0 %all-reduce.4.cloned.1.call-done = bf16[16,64,256]{2,1,0:T(8,128)(2,1)} async-done(((bf16[16,64,256]{2,1,0:T(8,128)(2,1)}), bf16[16,64,256]{2,1,0:T(8,128)(2,1)}) %all-reduce.4.cloned.1.call-update) | async-done | bytes 524304 | tf_op jit(solution)/shard_map/psum | solution.py:135
  142.7 1.9 %copy.62 = bf16[16,64,256]{2,1,0:T(8,128)(2,1)} copy(bf16[16,64,256]{2,1,0:T(8,128)(2,1)} %all-reduce.4.cloned.1.call-done) | data formatting | bytes 1048576
  (111 shorter events, 8.0 us)
Async XLA Ops:
  6.5 5.3 %copy-start = (bf16[2048,128]{1,0:T(8,128)(2,1)S(1)}, bf16[2048,128]{1,0:T(8,128)(2,1)}, u32[]{:S(2)}) copy-start(bf16[2048,128]{1,0:T(8,128)(2,1)} %param.17) | copy-start | bytes 1572868
  6.5 2.2 %copy-start.5 = (s32[2048,1]{0,1:T(1,128)S(1)}, s32[2048,1]{0,1:T(1,128)}, u32[]{:S(2)}) copy-start(s32[2048,1]{0,1:T(1,128)} %param.18) | copy-start | bytes 24580
  6.5 2.3 %copy-start.8 = (s32[2048]{0:T(1024)S(1)}, s32[2048]{0:T(1024)}, u32[]{:S(2)}) copy-start(s32[2048]{0:T(1024)} %param.19) | copy-start | bytes 24580
  6.5 2.3 %copy-start.6 = (s32[2048]{0:T(1024)S(1)}, s32[2048]{0:T(1024)}, u32[]{:S(2)}) copy-start(s32[2048]{0:T(1024)} %param.20) | copy-start | bytes 24580
  14.9 8.5 %copy-start.7 = (s32[2048]{0:T(1024)S(1)}, s32[2048]{0:T(1024)}, u32[]{:S(2)}) copy-start(s32[2048]{0:T(1024)} %param.23) | copy-start | bytes 24580
  15.9 7.6 %copy-start.4 = (s32[2048]{0:T(1024)S(1)}, s32[2048]{0:T(1024)}, u32[]{:S(2)}) copy-start(s32[2048]{0:T(1024)} %param.22) | copy-start | bytes 24580
  15.9 7.6 %copy-start.10 = (bf16[2048,128]{1,0:T(8,128)(2,1)S(1)}, bf16[2048,128]{1,0:T(8,128)(2,1)}, u32[]{:S(2)}) copy-start(bf16[2048,128]{1,0:T(8,128)(2,1)} %param.21) | copy-start | bytes 1572868
  15.9 22.6 %all-to-all-start = ((bf16[8,272,128]{2,1,0:T(8,128)(2,1)}), bf16[8,272,128]{2,1,0:T(8,128)(2,1)S(1)}, u32[]{:S(2)}, u32[]{:S(2)}) async-start(bf16[8,272,128]{2,1,0:T(8,128)(2,1)} %maximum_maximum_fusion), calls=%async_computation | async-start | bytes 1114112 | tf_op jit(solution)/shard_map/all_to_all | solution.py:91
  23.3 119.4 %all-reduce.4.cloned.1.call-start = ((), (), s32[]{:S(2)}) async-start(), calls=%async_computation.1 | async-start | bytes 1048576 | tf_op jit(solution)/shard_map/psum | solution.py:135
  49.4 0.7 copy-start.9
  50.3 6.8 %collective-permute-start = (bf16[3,256,128]{2,1,0:T(8,128)(2,1)S(1)}, bf16[3,256,128]{2,1,0:T(8,128)(2,1)S(1)}, u32[]{:S(2)}, u32[]{:S(2)}) collective-permute-start(bf16[3,256,128]{2,1,0:T(8,128)(2,1)S(1)} %bitcast.157), channel_id=1, source_target_pairs={{0,1},{1,2},{2,3},{3,4},{4,5},{5,6},{6,7},{8,9},{9,10},{10,11},{11... | collective-permute-start | bytes 589832 | tf_op jit(solution)/shard_map/ppermute | solution.py:14
  60.9 1.0 copy-start.3
  63.0 0.7 copy-start.13
  64.9 1.1 copy-start.2
  66.3 0.9 copy-start.11
  66.3 0.9 copy-start.12
  67.9 0.8 copy-start.1
Sparse Core Ops, SparseCore 0:
  68.8 73.8 all-reduce.3
where the time goes:
time: 152 us; the launch traced here: 151 us
  waiting for transfers between devices  81 us (53%)
  matrix products  18.2 us (12%)
  local copies, waits for them, and re-layouts  14.9 us (10%)
  between operations  14.1 us (9%)
  other arithmetic  11.9 us (8%)
  starting transfers between devices  11 us (7%)
    psum x1, waiting for transfers between devices, body(): gathered = lax.psum(full, 'band')  74 us
    all_to_all x1, starting transfers between devices, route(): lax.all_to_all(packet, 'band', split_axis=0, concat_axis=0, tiled=True)  7.41 us
    dot_general x8, matrix products, one_block(): sums = jnp.dot(table, values, preferred_element_type=jnp.float32)  6.09 us
    unnamed x49, local copies, waits for them, and re-layouts  5.18 us
    add x8, other arithmetic, one_block(): ids = start + jnp.arange(block, dtype=jnp.int32)  5.01 us
    dynamic_slice x8, local copies, waits for them, and re-layouts, deposit(): sums, density = lax.map(one_block, starts)  4.82 us
    all_to_all x1, waiting for transfers between devices, route(): lax.all_to_all(packet, 'band', split_axis=0, concat_axis=0, tiled=True)  4.57 us
    reduce_sum x8, other arithmetic, one_block(): density = jnp.sum(table, axis=1, dtype=jnp.float32)  4.39 us
  transfers between devices with their start and end apart: 3, of which 3 were waited for; matrix products, arithmetic and copies ran while one was open for 7% of the time, Pallas kernels for 0%

commit v1 on v0

--- a/solution.py
+++ b/solution.py
@@ -6,6 +6,11 @@
 LAT_DEV = 8
 LON = 256
 META = 16
+
+
+def raise_tables(xs):
+    w2 = jax.lax.all_gather(xs, axis_name="band")
+    return jnp.sum(w2, axis=0)
 
 
 def passed_along(value, axis, by):
@@ -132,7 +137,7 @@
     mine = project(latent, proj_weight)
     full = jnp.zeros((bands,) + mine.shape, mine.dtype)
     full = lax.dynamic_update_slice(full, mine[None], (position_index, 0, 0, 0))
-    gathered = lax.psum(full, "band")
+    gathered = raise_tables(full)
     return gathered.reshape((bands * mine.shape[0],) + mine.shape[1:])
 
 

time: 152 us -> 154 us (1.013)
  other arithmetic: 11.9 us -> 16.5 us
  local copies, waits for them, and re-layouts: 14.9 us -> 12.3 us
    psum x1 -> x0, waiting for transfers between devices: 74 us -> none  [body(): gathered = lax.psum(full, 'band')]
    all_gather x0 -> x1, waiting for transfers between devices: none -> 73.9 us  [raise_tables(): w2 = jax.lax.all_gather(xs, axis_name='band')]
    reduce_sum x0 -> x1, other arithmetic: none -> 3.85 us  [raise_tables(): return jnp.sum(w2, axis=0)]
    unnamed x49 -> x46, local copies, waits for them, and re-layouts: 5.18 us -> 2.4 us
where the time goes in v1:
time: 154 us; the launch traced here: 153 us
  waiting for transfers between devices  80.9 us (53%)
  matrix products  18.2 us (12%)
  other arithmetic  16.5 us (11%)
  between operations  14.1 us (9%)
  local copies, waits for them, and re-layouts  12.3 us (8%)
  starting transfers between devices  10.9 us (7%)
    all_gather x1, waiting for transfers between devices, raise_tables(): w2 = jax.lax.all_gather(xs, axis_name='band')  73.9 us
    all_to_all x1, starting transfers between devices, route(): lax.all_to_all(packet, 'band', split_axis=0, concat_axis=0, tiled=True)  7.29 us
    dot_general x8, matrix products, one_block(): sums = jnp.dot(table, values, preferred_element_type=jnp.float32)  6.09 us
    dynamic_slice x8, local copies, waits for them, and re-layouts, deposit(): sums, density = lax.map(one_block, starts)  5.03 us
    add x8, other arithmetic, one_block(): ids = start + jnp.arange(block, dtype=jnp.int32)  5.03 us
    all_to_all x1, waiting for transfers between devices, route(): lax.all_to_all(packet, 'band', split_axis=0, concat_axis=0, tiled=True)  4.41 us
    reduce_sum x8, other arithmetic, one_block(): density = jnp.sum(table, axis=1, dtype=jnp.float32)  4.39 us
    reduce_sum x1, other arithmetic, raise_tables(): return jnp.sum(w2, axis=0)  3.85 us
  transfers between devices with their start and end apart: 3, of which 3 were waited for; matrix products, arithmetic and copies ran while one was open for 7% of the time, Pallas kernels for 0%

profile of v1, /device:TPU:0, one launch (start us, length us, event | category | flops | bytes accessed | tf_op | source)
XLA Modules:
  0.0 153.2 jit_solution(16907703933702470307)
XLA Ops:
  6.5 0.8 add_convert_fusion.1
  7.3 2.2 %fusion.30 = f32[2048]{0:T(1024)S(1)} fusion(s32[2048]{0:T(1024)} %bitcast.177), kind=kOutput, calls=%fused_computation.58 | convolution fusion | flops 71399424 | bytes 16384 | tf_op jit(solution)/shard_map/dot_general | solution.py:85
  9.6 2.9 %fusion.23 = bf16[3,2048]{1,0:T(4,128)(2,1)S(1)} fusion(s32[2048]{0:T(1024)S(1)} %convert_add_fusion, bf16[1,2048]{1,0:T(2,128)(2,1)S(1)} %stack.18, bf16[1,2048]{1,0:T(2,128)(2,1)S(1)} %stack.17, bf16[1,2048]{1,0:T(2,128)(2,1)S(1)} %stack.16), kind=kOutput, calls=%fused_computation.33 | convolution fusion | flops 29403136 | bytes 32768 | tf_op jit(solution)/shard_map/dot_general | solution.py:91
  12.6 3.0 %fusion.21 = bf16[2048,128]{1,0:T(8,128)(2,1)S(1)} fusion(bf16[2048,128]{1,0:T(8,128)(2,1)S(1)} %copy-done, s32[2048]{0:T(1024)S(1)} %convert_add_fusion), kind=kOutput, calls=%fused_computation.31 | convolution fusion | flops 1078198272 | bytes 1056768 | tf_op jit(solution)/shard_map/dot_general | solution.py:89
  15.7 1.0 maximum_maximum_fusion
  16.7 7.3 %all-to-all-start = ((bf16[8,272,128]{2,1,0:T(8,128)(2,1)}), bf16[8,272,128]{2,1,0:T(8,128)(2,1)S(1)}, u32[]{:S(2)}, u32[]{:S(2)}) async-start(bf16[8,272,128]{2,1,0:T(8,128)(2,1)} %maximum_maximum_fusion), calls=%async_computation | async-start | bytes 1114112 | tf_op jit(solution)/shard_map/all_to_all | solution.py:96
  24.1 10.6 %while.24 = (s32[]{:T(128)}, f32[4,512,128]{2,1,0:T(8,128)S(1)}, f32[4,512]{1,0:T(4,128)S(1)}, s32[4]{0:T(128)S(1)}, s32[2048]{0:T(1024)S(1)}, /*index=5*/bf16[2...) while((s32[]{:T(128)}, f32[4,512,128]{2,1,0:T(8,128)S(1)}, ...), condition=%wide.region_2.3_spmd, body=%wide.region_0.2_spmd.sunk | while | flops 274726912 | bytes 823421 | solution.py:40
  24.1 0.6 dynamic_slice.9
  24.8 0.6 iota_add_fusion.4
  25.4 0.5 convert_reduce_fusion.4
  26.0 0.8 fusion.198
  26.8 0.6 dynamic_slice.9
  27.4 0.6 iota_add_fusion.4
  28.0 0.5 convert_reduce_fusion.4
  28.6 0.8 fusion.198
  29.4 0.6 dynamic_slice.9
  30.0 0.6 iota_add_fusion.4
  30.7 0.5 convert_reduce_fusion.4
  31.3 0.8 fusion.198
  32.1 0.6 dynamic_slice.9
  32.7 0.6 iota_add_fusion.4
  33.3 0.5 convert_reduce_fusion.4
  33.9 0.8 fusion.198
  34.7 4.4 %all-to-all-done = bf16[8,272,128]{2,1,0:T(8,128)(2,1)S(1)} async-done(((bf16[8,272,128]{2,1,0:T(8,128)(2,1)}), bf16[8,272,128]{2,1,0:T(8,128)(2,1)S(1)}, u32[]{:S(2)}, u32[]{:S(2)}) %all-to-all-start) | async-done | bytes 557088 | tf_op jit(solution)/shard_map/all_to_all | solution.py:96
  39.4 10.6 %while.25 = (s32[]{:T(128)}, f32[4,512,128]{2,1,0:T(8,128)S(1)}, f32[4,512]{1,0:T(4,128)S(1)}, s32[4]{0:T(128)S(1)}, s32[2048]{0:T(1024)S(1)}, /*index=5*/bf16[2...) while((s32[]{:T(128)}, f32[4,512,128]{2,1,0:T(8,128)S(1)}, ...), condition=%wide.region_6.7_spmd, body=%wide.region_4.6_spmd.sunk | while | flops 274726912 | bytes 823421 | solution.py:40
  39.4 0.6 dynamic_slice.10
  40.0 0.6 iota_add_fusion.5
  40.7 0.5 convert_reduce_fusion.5
  41.3 0.8 fusion.200
  42.0 0.6 dynamic_slice.10
  42.7 0.6 iota_add_fusion.5
  43.9 0.8 fusion.200
  44.7 0.6 dynamic_slice.10
  45.3 0.6 iota_add_fusion.5
  46.6 0.8 fusion.200
  47.4 0.6 dynamic_slice.10
  48.0 0.6 iota_add_fusion.5
  49.2 0.8 fusion.200
  50.9 3.6 %collective-permute-start = (bf16[3,256,128]{2,1,0:T(8,128)(2,1)S(1)}, bf16[3,256,128]{2,1,0:T(8,128)(2,1)S(1)}, u32[]{:S(2)}, u32[]{:S(2)}) collective-permute-start(bf16[3,256,128]{2,1,0:T(8,128)(2,1)S(1)} %bitcast.156), channel_id=1, source_target_pairs={{0,1},{1,2},{2,3},{3,4},{4,5},{5,6},{6,7},{8,9},{9,10},{10,11},{11... | collective-permute-start | bytes 589832 | tf_op jit(solution)/shard_map/ppermute | solution.py:19
  54.5 0.7 add_convert_fusion
  55.2 2.5 %collective-permute-done = bf16[3,256,128]{2,1,0:T(8,128)(2,1)S(1)} collective-permute-done((bf16[3,256,128]{2,1,0:T(8,128)(2,1)S(1)}, bf16[3,256,128]{2,1,0:T(8,128)(2,1)S(1)}, u32[]{:S(2)}, u32[]{:S(2)}) %collective-permute-start) | collective-permute-done | bytes 196640 | tf_op jit(solution)/shard_map/ppermute | solution.py:19
  58.2 3.2 %fusion.169 = (bf16[5,1,128,1,128]{4,3,2,1,0:T(2,128)(2,1)S(1)}, bf16[5,1,128,1,128]{4,3,2,1,0:T(2,128)(2,1)S(1)}, bf16[5,1,128,1,128]{4,3,2,1,0:T(2,128)(2,1)S(...) fusion(bf16[6,2,129,2,128]{4,3,2,1,0:T(2,128)(2,1)S(1)} %reshap, ...), kind=kLoop, calls=%fused_computation.236 | loop fusion | bytes 2949120 | tf_op jit(solution)/shard_map/slice | solution.py:53
  61.7 0.7 copy-done.3
  63.9 0.9 fusion.37
  67.1 0.6 convolution_convert_fusion
  67.8 0.8 copy-done.1
  68.6 73.9 %all-gather.2.cloned.1.call-done = bf16[8,8,2,64,256]{4,3,2,1,0:T(8,128)(2,1)} async-done(((bf16[1,8,2,64,256]{4,3,2,1,0:T(8,128)(2,1)}), bf16[8,8,2,64,256]{4,3,2,1,0:T(8,128)(2,1)}) %all-gather.2.cloned.1.call-update) | async-done | bytes 4194320 | tf_op jit(solution)/shard_map/all_gather | solution.py:12
  142.5 3.8 %reduce_sum.40 = bf16[8,2,64,256]{3,2,1,0:T(8,128)(2,1)} reduce(bf16[8,8,2,64,256]{4,3,2,1,0:T(8,128)(2,1)} %all-gather.2.cloned.1.call-done, bf16[]{:T(256)} %constant.62.clone.1), dimensions={0}, to_apply=%region_7.8 | reduce | flops 1835008 | bytes 4718594 | tf_op jit(solution)/shard_map/reduce_sum | solution.py:13
  (109 shorter events, 7.8 us)
Async XLA Ops:
  6.5 6.0 %copy-start = (bf16[2048,128]{1,0:T(8,128)(2,1)S(1)}, bf16[2048,128]{1,0:T(8,128)(2,1)}, u32[]{:S(2)}) copy-start(bf16[2048,128]{1,0:T(8,128)(2,1)} %param.17) | copy-start | bytes 1572868
  7.3 2.2 %copy-start.5 = (s32[2048,1]{0,1:T(1,128)S(1)}, s32[2048,1]{0,1:T(1,128)}, u32[]{:S(2)}) copy-start(s32[2048,1]{0,1:T(1,128)} %param.18) | copy-start | bytes 24580
  7.3 2.3 %copy-start.7 = (s32[2048]{0:T(1024)S(1)}, s32[2048]{0:T(1024)}, u32[]{:S(2)}) copy-start(s32[2048]{0:T(1024)} %param.19) | copy-start | bytes 24580
  15.6 8.5 %copy-start.6 = (s32[2048]{0:T(1024)S(1)}, s32[2048]{0:T(1024)}, u32[]{:S(2)}) copy-start(s32[2048]{0:T(1024)} %param.23) | copy-start | bytes 24580
  15.6 8.6 %copy-start.4 = (s32[2048]{0:T(1024)S(1)}, s32[2048]{0:T(1024)}, u32[]{:S(2)}) copy-start(s32[2048]{0:T(1024)} %param.22) | copy-start | bytes 24580
  15.6 8.6 %copy-start.9 = (bf16[2048,128]{1,0:T(8,128)(2,1)S(1)}, bf16[2048,128]{1,0:T(8,128)(2,1)}, u32[]{:S(2)}) copy-start(bf16[2048,128]{1,0:T(8,128)(2,1)} %param.21) | copy-start | bytes 1572868
  16.7 22.5 %all-to-all-start = ((bf16[8,272,128]{2,1,0:T(8,128)(2,1)}), bf16[8,272,128]{2,1,0:T(8,128)(2,1)S(1)}, u32[]{:S(2)}, u32[]{:S(2)}) async-start(bf16[8,272,128]{2,1,0:T(8,128)(2,1)} %maximum_maximum_fusion), calls=%async_computation | async-start | bytes 1114112 | tf_op jit(solution)/shard_map/all_to_all | solution.py:96
  23.9 118.6 %all-gather.2.cloned.1.call-start = ((), (), s32[]{:S(2)}) async-start(), calls=%async_computation.1 | async-start | bytes 4718592 | tf_op jit(solution)/shard_map/all_gather | solution.py:12
  50.0 0.7 copy-start.8
  50.9 6.8 %collective-permute-start = (bf16[3,256,128]{2,1,0:T(8,128)(2,1)S(1)}, bf16[3,256,128]{2,1,0:T(8,128)(2,1)S(1)}, u32[]{:S(2)}, u32[]{:S(2)}) collective-permute-start(bf16[3,256,128]{2,1,0:T(8,128)(2,1)S(1)} %bitcast.156), channel_id=1, source_target_pairs={{0,1},{1,2},{2,3},{3,4},{4,5},{5,6},{6,7},{8,9},{9,10},{10,11},{11... | collective-permute-start | bytes 589832 | tf_op jit(solution)/shard_map/ppermute | solution.py:19
  61.5 1.0 copy-start.3
  63.0 0.9 copy-start.12
  64.8 1.1 copy-start.2
  65.6 1.5 copy-start.10
  65.6 1.5 copy-start.11
  67.7 0.8 copy-start.1
Sparse Core Ops, SparseCore 0:
  68.7 73.7 all-gather.1
